TPU v7x, 32 devices: a whole 2x2x4 slice. The times are simulated.
32 devices in a mesh: dp: 8 (over y, x, core), tensor: 4 (over z).
Axes of the slice: x: 2, y: 2, z: 4, core: 2. Of those that a mesh axis runs over, the one named last changes fastest.
Arguments:
- glu_input: bfloat16 [16, 256, 3072], P('dp', 'tensor'), may hold values from -12 to 12
- depth_kernel: float32 [31, 1536], replicated, may hold values from -1 to 1
- norm_scale: float32 [1536], replicated, may hold values from 0.5 to 1.5
- norm_shift: float32 [1536], replicated, may hold values from -3 to 3
- proj_weight: bfloat16 [1536, 1536], P('tensor'), may hold values from -0.15625 to 0.15625
- out_grad: bfloat16 [16, 256, 1536], P('dp', 'tensor'), may hold values from -6 to 6
Outputs:
- conv_output: bfloat16 [16, 256, 1536], P('dp', 'tensor')
- input_grad: bfloat16 [16, 256, 3072], P('dp', 'tensor')
- weight_grad: float32 [1536, 1536], P('tensor')
- kernel_grad: float32 [31, 1536], replicated
- scale_grad: float32 [1536], replicated
- shift_grad: float32 [1536], replicated
All inputs are finite; a program needn't handle non-finite values.
Results may differ from a plain program's by a relative error of at most 0.0057.
Values may be sent and summed in bfloat16 or wider, within the bound.
No kernel may reach another device: no remote copies, remote signals or barrier semaphores. Data moves between devices by JAX's collectives and lax.ppermute only.
A program may use at most 128 MiB of HBM per device.

v0:
```python
import jax
import jax.numpy as jnp
from jax import lax
from jax.sharding import PartitionSpec as P

epsilon = 1e-05


def extended(array, sides, width):
    for axis, dim in sides:
        peers, length = (lax.axis_size(axis), array.shape[dim])
        up = [(i, (i + 1) % peers) for i in range(peers - 1)]
        down = [(j, i) for i, j in up]
        last = lax.slice_in_dim(array, length - width, length, axis=dim)
        leading = lax.slice_in_dim(array, 0, width, axis=dim)
        before = lax.ppermute(last, axis, up)
        after = lax.ppermute(leading, axis, down)
        array = jnp.concatenate([before, array, after], axis=dim)
    return array


def is_power_of_two(n):
    return n > 0 and n & n - 1 == 0


def all_sum(x, axes):
    for axis in axes:
        peers = lax.axis_size(axis)
        if not is_power_of_two(peers):
            x = lax.psum(x, axis)
            continue
        step = 1
        while step < peers:
            x = x + lax.ppermute(x, axis, [(i, i ^ step) for i in range(peers)])
            step *= 2
    return x


def all_moments(mean, spread, count, axes):
    for axis in axes:
        peers = lax.axis_size(axis)
        step = 1
        while step < peers:
            other = lax.ppermute(
                jnp.stack([mean, spread]), axis, [(i, i ^ step) for i in range(peers)]
            )
            delta = other[0] - mean
            mean = (mean + other[0]) * 0.5
            spread = spread + other[1] + delta * delta * (count * 0.5)
            count = count * 2
            step *= 2
    return (mean, spread)


def rows_sum(x, axis):
    peers = lax.axis_size(axis)
    if not is_power_of_two(peers) or x.shape[0] % peers:
        return lax.psum(x, axis)
    me = lax.axis_index(axis)
    bits = []
    step = 1
    while step < peers:
        bit = lax.rem(me // step, 2)
        half = x.shape[0] // 2
        keep = lax.dynamic_slice_in_dim(x, bit * half, half, axis=0)
        give = lax.dynamic_slice_in_dim(x, (1 - bit) * half, half, axis=0)
        x = keep + lax.ppermute(give, axis, [(i, i ^ step) for i in range(peers)])
        bits.append((step, bit))
        step *= 2
    for step, bit in reversed(bits):
        other = lax.ppermute(x, axis, [(i, i ^ step) for i in range(peers)])
        x = jnp.where(bit == 0, jnp.concatenate([x, other]), jnp.concatenate([other, x]))
    return x


def gather_weight(block):
    if lax.axis_size("dp") % 2:
        return lax.all_gather(block, "tensor", axis=0, tiled=True)
    peers = lax.axis_size("tensor")
    half = block.shape[0] // 2
    core = lax.rem(lax.axis_index("dp"), 2)
    mine = lax.dynamic_slice_in_dim(block, core * half, half, axis=0)
    held = lax.all_gather(mine, "tensor", axis=0, tiled=False)
    other = lax.ppermute(held, "dp", [(i, i ^ 1) for i in range(lax.axis_size("dp"))])
    first = jnp.where(core == 0, held, other)
    second = jnp.where(core == 0, other, held)
    return jnp.concatenate([first, second], axis=1).reshape(peers * block.shape[0], block.shape[1])


def on_device(glu_input, depth_kernel, norm_scale, norm_shift, proj_weight, out_grad):
    width = proj_weight.shape[1]
    rows = proj_weight.shape[0]
    frames = glu_input.shape[1]
    taps = depth_kernel.shape[0]
    radius = (taps - 1) // 2
    peers = lax.axis_size("tensor")
    me = lax.axis_index("tensor")
    local = glu_input.shape[0] * frames
    everyone = local * lax.axis_size("dp") * peers
    flat_grad = out_grad.reshape(-1, width)
    group_grad = lax.all_gather(flat_grad, "tensor", axis=0, tiled=True)
    values = glu_input[..., :width].astype(jnp.float32)
    gates = jax.nn.sigmoid(glu_input[..., width:].astype(jnp.float32))
    gated = (values * gates).astype(jnp.bfloat16)
    padded = extended(gated, (("tensor", 1),), radius)
    conv_out = jnp.zeros(gated.shape, jnp.float32)
    for offset in range(taps):
        conv_out = conv_out + depth_kernel[offset] * padded[:, offset : offset + frames, :]
    mean_local = jnp.sum(conv_out, axis=(0, 1)) / local
    dev_local = conv_out - mean_local
    spread_local = jnp.sum(dev_local * dev_local, axis=(0, 1))
    if all((is_power_of_two(lax.axis_size(a)) for a in ("dp", "tensor"))):
        average, spread = all_moments(mean_local, spread_local, float(local), ("dp", "tensor"))
        variance = spread / everyone
    else:
        average = lax.psum(jnp.sum(conv_out, axis=(0, 1)), ("dp", "tensor")) / everyone
        centred0 = conv_out - average
        variance = lax.psum(jnp.sum(centred0 * centred0, axis=(0, 1)), ("dp", "tensor")) / everyone
    group_grad, average = lax.optimization_barrier((group_grad, average))
    own_columns = jnp.einsum(
        "fd,cd->fc", group_grad, proj_weight, preferred_element_type=jnp.float32
    )
    grad_act = lax.all_to_all(own_columns, "tensor", split_axis=0, concat_axis=1, tiled=True)
    grad_act = grad_act.reshape(out_grad.shape)
    centred = conv_out - average
    inverse = lax.rsqrt(variance + epsilon)
    normed = centred * inverse
    affine = norm_scale * normed + norm_shift
    sig_affine = jax.nn.sigmoid(affine)
    activated = (affine * sig_affine).astype(jnp.bfloat16)
    flat_act = activated.reshape(-1, width)
    group_act = lax.all_to_all(flat_act, "tensor", split_axis=1, concat_axis=0, tiled=True)
    local_grad = jnp.einsum("fc,fd->cd", group_act, group_grad, preferred_element_type=jnp.float32)
    grad_affine = grad_act * (sig_affine + affine * sig_affine * (1.0 - sig_affine))
    sums = jnp.stack(
        [jnp.sum(grad_affine, axis=(0, 1)), jnp.sum(grad_affine * normed, axis=(0, 1))]
    )
    sums = all_sum(sums, ("tensor", "dp"))
    shift_grad, scale_grad = (sums[0], sums[1])
    grad_conv = (
        norm_scale
        * inverse
        * (grad_affine - shift_grad / everyone - normed * scale_grad / everyone)
    ).astype(jnp.bfloat16)
    grad_pad = extended(grad_conv, (("tensor", 1),), radius)
    grad_gated = jnp.zeros(gated.shape, jnp.float32)
    for offset in range(taps):
        begin = 2 * radius - offset
        grad_gated = grad_gated + depth_kernel[offset] * grad_pad[:, begin : begin + frames, :]
    grad_wide = grad_conv.astype(jnp.float32)
    kernel_terms = jnp.stack(
        [
            jnp.sum(
                padded[:, offset : offset + frames, :].astype(jnp.float32) * grad_wide, axis=(0, 1)
            )
            for offset in range(taps)
        ]
    )
    weight_grad = rows_sum(local_grad, "dp")
    kernel_grad = all_sum(kernel_terms, ("dp", "tensor"))
    input_grad = jnp.concatenate(
        [grad_gated * gates, grad_gated * values * gates * (1.0 - gates)], axis=-1
    ).astype(jnp.bfloat16)
    full_weight = gather_weight(proj_weight)
    conv_output = jnp.einsum(
        "btc,cd->btd", activated, full_weight, preferred_element_type=jnp.float32
    ).astype(jnp.bfloat16)
    return (conv_output, input_grad, weight_grad, kernel_grad, scale_grad, shift_grad)


def solution(mesh):
    in_specs = (P("dp", "tensor", None), P(), P(), P(), P("tensor", None), P("dp", "tensor", None))
    out_specs = (P("dp", "tensor", None), P("dp", "tensor", None), P("tensor", None), P(), P(), P())
    return jax.shard_map(
        on_device, mesh=mesh, in_specs=in_specs, out_specs=out_specs, check_vma=False
    )
```

profile of v0, /device:TPU:0, one launch (start us, length us, event | category | flops | bytes accessed | tf_op | source)
XLA Modules:
  0.0 186.6 jit_solution(8996814178643198088)
XLA Ops:
  9.3 4.9 %collective-permute-start = (bf16[2,15,1536]{2,1,0:T(8,128)(2,1)S(1)}, bf16[2,15,1536]{2,1,0:T(8,128)(2,1)S(1)}, u32[]{:S(2)}, u32[]{:S(2)}) collective-permute-start(bf16[2,15,1536]{2,1,0:T(8,128)(2,1)S(1)} %get-tuple-element.99), channel_id=1, source_target_pairs={{0,1},{1,2},{2,3},{4,5},{5,6},{6,7},{8,9},{9,10},{10,11},{12,13},{... | collective-permute-start | bytes 276488 | tf_op jit(solution)/shard_map/ppermute | solution.py:16
  16.4 4.3 %collective-permute-done.1 = bf16[2,15,1536]{2,1,0:T(8,128)(2,1)S(1)} collective-permute-done((bf16[2,15,1536]{2,1,0:T(8,128)(2,1)S(1)}, bf16[2,15,1536]{2,1,0:T(8,128)(2,1)S(1)}, u32[]{:S(2)}, u32[]{:S(2)}) %collective-permute-start.1) | collective-permute-done | bytes 92192 | tf_op jit(solution)/shard_map/ppermute | solution.py:17
  20.7 3.8 %fusion.143 = (f32[1536]{0:T(1024)S(1)}, f32[2,64,1536]{2,1,0:T(8,128)S(1)}) fusion(bf16[2,15,1536]{2,1,0:T(8,128)(2,1)S(1)} %collective-permute-done.1, bf16[2,64,1536]{2,1,0:T(8,128)(2,1)S(1)} %fusion, f32[1536]{0:T(1024)S(1)} %get-tuple-element.72, f32[1536]{0:T(1024)S(1)} %get-tuple-element.73, f32[1536]{0:T(1024)S(1)} %get-tuple-element.44, ...), kind=kLoop, calls=%fused_computation.380 | loop fusion | flops 35977728 | bytes 1560576 | tf_op jit(solution)/shard_map/reduce_sum | solution.py:109
  26.1 1.6 collective-permute-start.3
  27.7 2.2 %collective-permute-done.3 = f32[2,1536]{1,0:T(2,128)S(1)} collective-permute-done((f32[2,1536]{1,0:T(2,128)S(1)}, f32[2,1536]{1,0:T(2,128)S(1)}, u32[]{:S(2)}, u32[]{:S(2)}) %collective-permute-start.3) | collective-permute-done | bytes 12320 | tf_op jit(solution)/shard_map/ppermute | solution.py:44
  29.9 1.6 collective-permute-start.4
  31.5 2.2 %collective-permute-done.4 = f32[2,1536]{1,0:T(2,128)S(1)} collective-permute-done((f32[2,1536]{1,0:T(2,128)S(1)}, f32[2,1536]{1,0:T(2,128)S(1)}, u32[]{:S(2)}, u32[]{:S(2)}) %collective-permute-start.4) | collective-permute-done | bytes 12320 | tf_op jit(solution)/shard_map/ppermute | solution.py:44
  33.8 1.6 collective-permute-start.5
  35.4 2.5 %collective-permute-done.5 = f32[2,1536]{1,0:T(2,128)S(1)} collective-permute-done((f32[2,1536]{1,0:T(2,128)S(1)}, f32[2,1536]{1,0:T(2,128)S(1)}, u32[]{:S(2)}, u32[]{:S(2)}) %collective-permute-start.5) | collective-permute-done | bytes 12320 | tf_op jit(solution)/shard_map/ppermute | solution.py:44
  38.0 2.5 %collective-permute-start.6 = (f32[2,1536]{1,0:T(2,128)S(1)}, f32[2,1536]{1,0:T(2,128)S(1)}, u32[]{:S(2)}, u32[]{:S(2)}) collective-permute-start(f32[2,1536]{1,0:T(2,128)S(1)} %pad_maximum_fusion.10), channel_id=1, source_target_pairs={{0,2},{1,3},{2,0},{3,1},{4,6},{5,7},{6,4},{7,5},{8,10},{9,11},{10,... | collective-permute-start | bytes 36872 | tf_op jit(solution)/shard_map/ppermute | solution.py:44
  40.5 2.9 %collective-permute-done.6 = f32[2,1536]{1,0:T(2,128)S(1)} collective-permute-done((f32[2,1536]{1,0:T(2,128)S(1)}, f32[2,1536]{1,0:T(2,128)S(1)}, u32[]{:S(2)}, u32[]{:S(2)}) %collective-permute-start.6) | collective-permute-done | bytes 12320 | tf_op jit(solution)/shard_map/ppermute | solution.py:44
  44.2 5.8 %all-gather.4.cloned.1.call-done = bf16[512,1536]{1,0:T(8,128)(2,1)} async-done(((bf16[128,1536]{1,0:T(8,128)(2,1)}), bf16[512,1536]{1,0:T(8,128)(2,1)}) %all-gather.4.cloned.1.call-update) | async-done | bytes 1572880 | tf_op jit(solution)/shard_map/all_gather | solution.py:101
  50.0 2.4 %fusion.147 = f32[512,384]{1,0:T(8,128)S(1)} fusion(bf16[512,1536]{1,0:T(8,128)(2,1)} %all-gather.4.cloned.1.call-done, bf16[384,1536]{1,0:T(8,128)(2,1)S(1)} %copy-done), kind=kOutput, calls=%fused_computation.383 | convolution fusion | flops 603979776 | bytes 3538944 | tf_op jit(solution)/shard_map/fd,cd->fc/dot_general | solution.py:120
  52.4 22.6 %all_to_all.35 = f32[4,128,384]{2,1,0:T(8,128)S(1)} all-to-all(f32[4,128,384]{2,1,0:T(8,128)S(1)} %bitcast.21), channel_id=1, replica_groups=mesh['dp'=8,'tensor'=4] {'tensor'}, dimensions={0} | all-to-all | bytes 1572864 | tf_op jit(solution)/shard_map/all_to_all | solution.py:123
  76.8 2.4 %fusion.140 = (f32[1536]{0:T(1024)S(1)}, f32[1536]{0:T(1024)S(1)}, f32[2,64,1536]{2,1,0:T(8,128)}, bf16[2,64,1536]{2,1,0:T(8,128)(2,1)S(1)}) fusion(f32[1536]{0:T(1024)S(1)} %get-tuple-element.90, f32[2,64,1536]{2,1,0:T(8,128)S(1)} %get-tuple-element.93, f32[1536]{0:T(1024)S(1)} %get-tuple-element.8, f32[2,64,1536]{2,1,0:T(8,128)} %reshape.189, ...), kind=kLoop, calls=%fused_computation.378 | loop fusion | flops 3142656 | bytes 2789376 | tf_op jit(solution)/shard_map/reduce_sum | solution.py:136
  80.4 3.5 %all-to-all-start.1 = ((bf16[128,4,384]{2,0,1:T(8,128)(2,1)}), bf16[128,4,384]{2,0,1:T(8,128)(2,1)S(1)}, u32[]{:S(2)}, u32[]{:S(2)}) async-start(bf16[128,4,384]{2,0,1:T(8,128)(2,1)} %copy.17), calls=%async_computation.1 | async-start | bytes 786432 | tf_op jit(solution)/shard_map/all_to_all | solution.py:132
  84.2 2.7 %collective-permute-start.9 = (f32[2,1536]{1,0:T(2,128)S(1)}, f32[2,1536]{1,0:T(2,128)S(1)}, u32[]{:S(2)}, u32[]{:S(2)}) collective-permute-start(f32[2,1536]{1,0:T(2,128)S(1)} %fusion.139), channel_id=1, source_target_pairs={{0,2},{1,3},{2,0},{3,1},{4,6},{5,7},{6,4},{7,5},{8,10},{9,11},{10,... | collective-permute-start | bytes 36872 | tf_op jit(solution)/shard_map/ppermute | solution.py:34
  87.8 7.6 %collective-permute-done.9 = f32[2,1536]{1,0:T(2,128)S(1)} collective-permute-done((f32[2,1536]{1,0:T(2,128)S(1)}, f32[2,1536]{1,0:T(2,128)S(1)}, u32[]{:S(2)}, u32[]{:S(2)}) %collective-permute-start.9) | collective-permute-done | bytes 12320 | tf_op jit(solution)/shard_map/ppermute | solution.py:34
  98.2 2.2 %collective-permute-done.11 = f32[2,1536]{1,0:T(2,128)S(1)} collective-permute-done((f32[2,1536]{1,0:T(2,128)S(1)}, f32[2,1536]{1,0:T(2,128)S(1)}, u32[]{:S(2)}, u32[]{:S(2)}) %collective-permute-start.11) | collective-permute-done | bytes 12320 | tf_op jit(solution)/shard_map/ppermute | solution.py:34
  102.0 2.2 %collective-permute-done.12 = f32[2,1536]{1,0:T(2,128)S(1)} collective-permute-done((f32[2,1536]{1,0:T(2,128)S(1)}, f32[2,1536]{1,0:T(2,128)S(1)}, u32[]{:S(2)}, u32[]{:S(2)}) %collective-permute-start.12) | collective-permute-done | bytes 12320 | tf_op jit(solution)/shard_map/ppermute | solution.py:34
  104.2 2.2 %fusion.148 = f32[384,1536]{1,0:T(8,128)S(1)} fusion(bf16[512,384]{1,0:T(8,128)(2,1)S(1)} %bitcast.20, bf16[512,1536]{1,0:T(8,128)(2,1)} %all-gather.4.cloned.1.call-done), kind=kOutput, calls=%fused_computation.384 | convolution fusion | flops 603979776 | bytes 4325376 | tf_op jit(solution)/shard_map/fc,fd->cd/dot_general | solution.py:133
  107.6 1.5 fusion.80
  121.1 2.5 %stack.172 = f32[31,1536]{1,0:T(8,128)S(1)} concatenate(f32[1,1536]{1,0:T(1,128)} %stack.141, f32[1,1536]{1,0:T(1,128)} %stack.142, f32[1,1536]{1,0:T(1,128)} %stack.143, f32[1,1536]{1,0:T(1,128)} %stack.144, f32[1,1536]{1,0:T(1,128)} %stack.145, f32[1,1536]{1,0:T(1,128)S(1)} %stack.146, f32[1,1536]{1,0:T(1,128)S(1)} %stack.147, f32[1,1536]{1,0:T(1,128)S(1)} %stack.148, ...), dimensions={0} | concatenate | bytes 380928 | tf_op jit(solution)/shard_map/stack | solution.py:151
  123.8 14.4 %all-gather.6.cloned.1.call-done = bf16[768,1536]{1,0:T(8,128)(2,1)} async-done(((bf16[192,1536]{1,0:T(8,128)(2,1)}), bf16[768,1536]{1,0:T(8,128)(2,1)}) %all-gather.6.cloned.1.call-update) | async-done | bytes 2359312 | tf_op jit(solution)/shard_map/all_gather | solution.py:83
  144.1 4.6 %collective-permute-start.14 = (bf16[2,15,1536]{2,1,0:T(8,128)(2,1)S(1)}, bf16[2,15,1536]{2,1,0:T(8,128)(2,1)S(1)}, u32[]{:S(2)}, u32[]{:S(2)}) collective-permute-start(bf16[2,15,1536]{2,1,0:T(8,128)(2,1)S(1)} %get-tuple-element.98), channel_id=1, source_target_pairs={{0,1},{1,2},{2,3},{4,5},{5,6},{6,7},{8,9},{9,10},{10,11},{12,13},{... | collective-permute-start | bytes 276488 | tf_op jit(solution)/shard_map/ppermute | solution.py:16
  150.5 2.1 %collective-permute-start.18 = (f32[48,1536]{1,0:T(8,128)S(1)}, f32[48,1536]{1,0:T(8,128)S(1)}, u32[]{:S(2)}, u32[]{:S(2)}) collective-permute-start(f32[48,1536]{1,0:T(8,128)S(1)} %dynamic-slice_add_fusion.2), channel_id=1, source_target_pairs={{0,16},{4,20},{8,24},{12,28},{16,0},{20,4},{24,8},{28,12},{1,17},{... | collective-permute-start | bytes 884744 | tf_op jit(solution)/shard_map/ppermute | solution.py:71
  152.9 4.1 %multiply_convert_fusion = (bf16[2,64,1536]{2,1,0:T(8,128)(2,1)S(1)}, f32[2,64,1536]{2,1,0:T(8,128)S(1)}) fusion(bf16[2,64,3072]{2,1,0:T(8,128)(2,1)S(1)} %copy-done.1, bf16[2,64,1536]{2,1,0:T(8,128)(2,1)S(1)} %get-tuple-element.86, bf16[2,15,1536]{2,1,0:T(8,128)(2,1)S(1)} %collective-permute-done.14, f32[1536]{0:T(1024)S(1)} %copy-done.62, ...), kind=kLoop, calls=%fused_computation.210 | loop fusion | flops 36962304 | bytes 2340864 | tf_op jit(solution)/shard_map/convert
  157.7 3.6 %collective-permute-done.18 = f32[48,1536]{1,0:T(8,128)S(1)} collective-permute-done((f32[48,1536]{1,0:T(8,128)S(1)}, f32[48,1536]{1,0:T(8,128)S(1)}, u32[]{:S(2)}, u32[]{:S(2)}) %collective-permute-start.18) | collective-permute-done | bytes 294944 | tf_op jit(solution)/shard_map/ppermute | solution.py:71
  165.0 7.5 %collective-permute-done.25 = f32[31,1536]{1,0:T(8,128)S(1)} collective-permute-done((f32[31,1536]{1,0:T(8,128)S(1)}, f32[31,1536]{1,0:T(8,128)S(1)}, u32[]{:S(2)}, u32[]{:S(2)}) %collective-permute-start.25) | collective-permute-done | bytes 190496 | tf_op jit(solution)/shard_map/ppermute | solution.py:34
  173.2 1.9 %collective-permute-done.19 = f32[96,1536]{1,0:T(8,128)S(1)} collective-permute-done((f32[96,1536]{1,0:T(8,128)S(1)}, f32[96,1536]{1,0:T(8,128)S(1)}, u32[]{:S(2)}, u32[]{:S(2)}) %collective-permute-start.19) | collective-permute-done | bytes 589856 | tf_op jit(solution)/shard_map/ppermute | solution.py:71
  175.9 1.5 convolution_convert_fusion
  178.1 1.6 maximum_select_fusion
  (266 shorter events, 41.7 us)
Async XLA Ops:
  7.2 42.8 %copy-start = (bf16[384,1536]{1,0:T(8,128)(2,1)S(1)}, bf16[384,1536]{1,0:T(8,128)(2,1)}, u32[]{:S(2)}) copy-start(bf16[384,1536]{1,0:T(8,128)(2,1)} %param.10) | copy-start | bytes 3538948
  7.2 42.8 %all-gather.4.cloned.1.call-start = ((), (), s32[]{:S(2)}) async-start(), calls=%async_computation.2 | async-start | bytes 1966080 | tf_op jit(solution)/shard_map/all_gather | solution.py:101
  9.3 7.1 %collective-permute-start = (bf16[2,15,1536]{2,1,0:T(8,128)(2,1)S(1)}, bf16[2,15,1536]{2,1,0:T(8,128)(2,1)S(1)}, u32[]{:S(2)}, u32[]{:S(2)}) collective-permute-start(bf16[2,15,1536]{2,1,0:T(8,128)(2,1)S(1)} %get-tuple-element.99), channel_id=1, source_target_pairs={{0,1},{1,2},{2,3},{4,5},{5,6},{6,7},{8,9},{9,10},{10,11},{12,13},{... | collective-permute-start | bytes 276488 | tf_op jit(solution)/shard_map/ppermute | solution.py:16
  14.2 6.5 %collective-permute-start.1 = (bf16[2,15,1536]{2,1,0:T(8,128)(2,1)S(1)}, bf16[2,15,1536]{2,1,0:T(8,128)(2,1)S(1)}, u32[]{:S(2)}, u32[]{:S(2)}) collective-permute-start(bf16[2,15,1536]{2,1,0:T(8,128)(2,1)S(1)} %get-tuple-element.100), channel_id=1, source_target_pairs={{1,0},{2,1},{3,2},{5,4},{6,5},{7,6},{9,8},{10,9},{11,10},{13,12},{... | collective-permute-start | bytes 276488 | tf_op jit(solution)/shard_map/ppermute | solution.py:17
  16.3 36.0 %copy-start.45 = (f32[1536]{0:T(1024)}, f32[1536]{0:T(1024)S(1)}, u32[]{:S(2)}) copy-start(f32[1536]{0:T(1024)S(1)} %get-tuple-element.64) | copy-start | bytes 18436
  16.3 36.0 %copy-start.47 = (f32[1536]{0:T(1024)}, f32[1536]{0:T(1024)S(1)}, u32[]{:S(2)}) copy-start(f32[1536]{0:T(1024)S(1)} %get-tuple-element.65) | copy-start | bytes 18436
  24.8 1.2 collective-permute-start.2
  26.1 3.8 %collective-permute-start.3 = (f32[2,1536]{1,0:T(2,128)S(1)}, f32[2,1536]{1,0:T(2,128)S(1)}, u32[]{:S(2)}, u32[]{:S(2)}) collective-permute-start(f32[2,1536]{1,0:T(2,128)S(1)} %pad_maximum_fusion.7), channel_id=1, source_target_pairs={{0,8},{4,12},{8,0},{12,4},{16,24},{20,28},{24,16},{28,20},{1,9},{5... | collective-permute-start | bytes 36872 | tf_op jit(solution)/shard_map/ppermute | solution.py:44
  29.9 3.8 %collective-permute-start.4 = (f32[2,1536]{1,0:T(2,128)S(1)}, f32[2,1536]{1,0:T(2,128)S(1)}, u32[]{:S(2)}, u32[]{:S(2)}) collective-permute-start(f32[2,1536]{1,0:T(2,128)S(1)} %pad_maximum_fusion.8), channel_id=1, source_target_pairs={{0,16},{4,20},{8,24},{12,28},{16,0},{20,4},{24,8},{28,12},{1,17},{... | collective-permute-start | bytes 36872 | tf_op jit(solution)/shard_map/ppermute | solution.py:44
  33.8 4.2 %collective-permute-start.5 = (f32[2,1536]{1,0:T(2,128)S(1)}, f32[2,1536]{1,0:T(2,128)S(1)}, u32[]{:S(2)}, u32[]{:S(2)}) collective-permute-start(f32[2,1536]{1,0:T(2,128)S(1)} %pad_maximum_fusion.9), channel_id=1, source_target_pairs={{0,1},{1,0},{2,3},{3,2},{4,5},{5,4},{6,7},{7,6},{8,9},{9,8},{10,11... | collective-permute-start | bytes 36872 | tf_op jit(solution)/shard_map/ppermute | solution.py:44
  38.0 5.4 %collective-permute-start.6 = (f32[2,1536]{1,0:T(2,128)S(1)}, f32[2,1536]{1,0:T(2,128)S(1)}, u32[]{:S(2)}, u32[]{:S(2)}) collective-permute-start(f32[2,1536]{1,0:T(2,128)S(1)} %pad_maximum_fusion.10), channel_id=1, source_target_pairs={{0,2},{1,3},{2,0},{3,1},{4,6},{5,7},{6,4},{7,5},{8,10},{9,11},{10,... | collective-permute-start | bytes 36872 | tf_op jit(solution)/shard_map/ppermute | solution.py:44
  79.3 4.9 %collective-permute-start.8 = (f32[2,1536]{1,0:T(2,128)S(1)}, f32[2,1536]{1,0:T(2,128)S(1)}, u32[]{:S(2)}, u32[]{:S(2)}) collective-permute-start(f32[2,1536]{1,0:T(2,128)S(1)} %pad_maximum_fusion.11), channel_id=1, source_target_pairs={{0,1},{1,0},{2,3},{3,2},{4,5},{5,4},{6,7},{7,6},{8,9},{9,8},{10,11... | collective-permute-start | bytes 36872 | tf_op jit(solution)/shard_map/ppermute | solution.py:34
  80.4 23.8 %all-to-all-start.1 = ((bf16[128,4,384]{2,0,1:T(8,128)(2,1)}), bf16[128,4,384]{2,0,1:T(8,128)(2,1)S(1)}, u32[]{:S(2)}, u32[]{:S(2)}) async-start(bf16[128,4,384]{2,0,1:T(8,128)(2,1)} %copy.17), calls=%async_computation.1 | async-start | bytes 786432 | tf_op jit(solution)/shard_map/all_to_all | solution.py:132
  83.9 54.3 %all-gather.6.cloned.1.call-start = ((), (), s32[]{:S(2)}) async-start(), calls=%async_computation.3 | async-start | bytes 2949120 | tf_op jit(solution)/shard_map/all_gather | solution.py:83
  84.2 11.2 %collective-permute-start.9 = (f32[2,1536]{1,0:T(2,128)S(1)}, f32[2,1536]{1,0:T(2,128)S(1)}, u32[]{:S(2)}, u32[]{:S(2)}) collective-permute-start(f32[2,1536]{1,0:T(2,128)S(1)} %fusion.139), channel_id=1, source_target_pairs={{0,2},{1,3},{2,0},{3,1},{4,6},{5,7},{6,4},{7,5},{8,10},{9,11},{10,... | collective-permute-start | bytes 36872 | tf_op jit(solution)/shard_map/ppermute | solution.py:34
  95.4 1.2 collective-permute-start.10
  96.7 3.8 %collective-permute-start.11 = (f32[2,1536]{1,0:T(2,128)S(1)}, f32[2,1536]{1,0:T(2,128)S(1)}, u32[]{:S(2)}, u32[]{:S(2)}) collective-permute-start(f32[2,1536]{1,0:T(2,128)S(1)} %add.496), channel_id=1, source_target_pairs={{0,8},{4,12},{8,0},{12,4},{16,24},{20,28},{24,16},{28,20},{1,9},{5... | collective-permute-start | bytes 36872 | tf_op jit(solution)/shard_map/ppermute | solution.py:34
  100.5 3.8 %collective-permute-start.12 = (f32[2,1536]{1,0:T(2,128)S(1)}, f32[2,1536]{1,0:T(2,128)S(1)}, u32[]{:S(2)}, u32[]{:S(2)}) collective-permute-start(f32[2,1536]{1,0:T(2,128)S(1)} %add.497), channel_id=1, source_target_pairs={{0,16},{4,20},{8,24},{12,28},{16,0},{20,4},{24,8},{28,12},{1,17},{... | collective-permute-start | bytes 36872 | tf_op jit(solution)/shard_map/ppermute | solution.py:34
  106.6 3.8 %collective-permute-start.15 = (f32[192,1536]{1,0:T(8,128)S(1)}, f32[192,1536]{1,0:T(8,128)S(1)}, u32[]{:S(2)}, u32[]{:S(2)}) collective-permute-start(f32[192,1536]{1,0:T(8,128)S(1)} %constant_dynamic-slice_fusion.2), channel_id=1, source_target_pairs={{0,4},{4,0},{8,12},{12,8},{16,20},{20,16},{24,28},{28,24},{1,5},{5... | collective-permute-start | bytes 3538952 | tf_op jit(solution)/shard_map/ppermute | solution.py:67
  112.4 27.4 %collective-permute-start.16 = (f32[96,1536]{1,0:T(8,128)}, f32[96,1536]{1,0:T(8,128)}, u32[]{:S(2)}, u32[]{:S(2)}) collective-permute-start(f32[96,1536]{1,0:T(8,128)} %constant_dynamic-slice_fusion.1), channel_id=1, source_target_pairs={{0,8},{4,12},{8,0},{12,4},{16,24},{20,28},{24,16},{28,20},{1,9},{5... | collective-permute-start | bytes 1769480 | tf_op jit(solution)/shard_map/ppermute | solution.py:67
  123.6 14.6 %collective-permute-start.21 = (f32[31,1536]{1,0:T(8,128)S(1)}, f32[31,1536]{1,0:T(8,128)S(1)}, u32[]{:S(2)}, u32[]{:S(2)}) collective-permute-start(f32[31,1536]{1,0:T(8,128)S(1)} %stack.172), channel_id=1, source_target_pairs={{0,4},{4,0},{8,12},{12,8},{16,20},{20,16},{24,28},{28,24},{1,5},{5... | collective-permute-start | bytes 571400 | tf_op jit(solution)/shard_map/ppermute | solution.py:34
  138.2 37.1 %collective-permute-start.7 = (bf16[4,192,1536]{2,1,0:T(8,128)(2,1)}, bf16[4,192,1536]{2,1,0:T(8,128)(2,1)S(1)}, u32[]{:S(2)}, u32[]{:S(2)}) collective-permute-start(bf16[4,192,1536]{2,1,0:T(8,128)(2,1)} %bitcast.18), channel_id=1, source_target_pairs={{0,4},{4,0},{8,12},{12,8},{16,20},{20,16},{24,28},{28,24},{1,5},{5... | collective-permute-start | bytes 7077896 | tf_op jit(solution)/shard_map/ppermute | solution.py:84
  138.2 10.4 %collective-permute-start.22 = (f32[31,1536]{1,0:T(8,128)S(1)}, f32[31,1536]{1,0:T(8,128)S(1)}, u32[]{:S(2)}, u32[]{:S(2)}) collective-permute-start(f32[31,1536]{1,0:T(8,128)S(1)} %add.537), channel_id=1, source_target_pairs={{0,8},{4,12},{8,0},{12,4},{16,24},{20,28},{24,16},{28,20},{1,9},{5... | collective-permute-start | bytes 571400 | tf_op jit(solution)/shard_map/ppermute | solution.py:34
  141.2 9.2 %collective-permute-start.17 = (f32[48,1536]{1,0:T(8,128)S(1)}, f32[48,1536]{1,0:T(8,128)S(1)}, u32[]{:S(2)}, u32[]{:S(2)}) collective-permute-start(f32[48,1536]{1,0:T(8,128)S(1)} %constant_dynamic-slice_fusion), channel_id=1, source_target_pairs={{0,16},{4,20},{8,24},{12,28},{16,0},{20,4},{24,8},{28,12},{1,17},{... | collective-permute-start | bytes 884744 | tf_op jit(solution)/shard_map/ppermute | solution.py:67
  142.8 9.8 %collective-permute-start.13 = (bf16[2,15,1536]{2,1,0:T(8,128)(2,1)S(1)}, bf16[2,15,1536]{2,1,0:T(8,128)(2,1)S(1)}, u32[]{:S(2)}, u32[]{:S(2)}) collective-permute-start(bf16[2,15,1536]{2,1,0:T(8,128)(2,1)S(1)} %get-tuple-element.97), channel_id=1, source_target_pairs={{1,0},{2,1},{3,2},{5,4},{6,5},{7,6},{9,8},{10,9},{11,10},{13,12},{... | collective-permute-start | bytes 276488 | tf_op jit(solution)/shard_map/ppermute | solution.py:17
  144.1 8.5 %collective-permute-start.14 = (bf16[2,15,1536]{2,1,0:T(8,128)(2,1)S(1)}, bf16[2,15,1536]{2,1,0:T(8,128)(2,1)S(1)}, u32[]{:S(2)}, u32[]{:S(2)}) collective-permute-start(bf16[2,15,1536]{2,1,0:T(8,128)(2,1)S(1)} %get-tuple-element.98), channel_id=1, source_target_pairs={{0,1},{1,2},{2,3},{4,5},{5,6},{6,7},{8,9},{9,10},{10,11},{12,13},{... | collective-permute-start | bytes 276488 | tf_op jit(solution)/shard_map/ppermute | solution.py:16
  148.7 8.2 %collective-permute-start.23 = (f32[31,1536]{1,0:T(8,128)S(1)}, f32[31,1536]{1,0:T(8,128)S(1)}, u32[]{:S(2)}, u32[]{:S(2)}) collective-permute-start(f32[31,1536]{1,0:T(8,128)S(1)} %add.538), channel_id=1, source_target_pairs={{0,16},{4,20},{8,24},{12,28},{16,0},{20,4},{24,8},{28,12},{1,17},{... | collective-permute-start | bytes 571400 | tf_op jit(solution)/shard_map/ppermute | solution.py:34
  150.5 10.8 %collective-permute-start.18 = (f32[48,1536]{1,0:T(8,128)S(1)}, f32[48,1536]{1,0:T(8,128)S(1)}, u32[]{:S(2)}, u32[]{:S(2)}) collective-permute-start(f32[48,1536]{1,0:T(8,128)S(1)} %dynamic-slice_add_fusion.2), channel_id=1, source_target_pairs={{0,16},{4,20},{8,24},{12,28},{16,0},{20,4},{24,8},{28,12},{1,17},{... | collective-permute-start | bytes 884744 | tf_op jit(solution)/shard_map/ppermute | solution.py:71
  157.0 5.7 %collective-permute-start.24 = (f32[31,1536]{1,0:T(8,128)S(1)}, f32[31,1536]{1,0:T(8,128)S(1)}, u32[]{:S(2)}, u32[]{:S(2)}) collective-permute-start(f32[31,1536]{1,0:T(8,128)S(1)} %add.539), channel_id=1, source_target_pairs={{0,1},{1,0},{2,3},{3,2},{4,5},{5,4},{6,7},{7,6},{8,9},{9,8},{10,11... | collective-permute-start | bytes 571400 | tf_op jit(solution)/shard_map/ppermute | solution.py:34
  161.3 13.8 %collective-permute-start.19 = (f32[96,1536]{1,0:T(8,128)S(1)}, f32[96,1536]{1,0:T(8,128)S(1)}, u32[]{:S(2)}, u32[]{:S(2)}) collective-permute-start(f32[96,1536]{1,0:T(8,128)S(1)} %maximum_select_fusion.2), channel_id=1, source_target_pairs={{0,8},{4,12},{8,0},{12,4},{16,24},{20,28},{24,16},{28,20},{1,9},{5... | collective-permute-start | bytes 1769480 | tf_op jit(solution)/shard_map/ppermute | solution.py:71
  162.7 9.7 %collective-permute-start.25 = (f32[31,1536]{1,0:T(8,128)S(1)}, f32[31,1536]{1,0:T(8,128)S(1)}, u32[]{:S(2)}, u32[]{:S(2)}) collective-permute-start(f32[31,1536]{1,0:T(8,128)S(1)} %add.540), channel_id=1, source_target_pairs={{0,2},{1,3},{2,0},{3,1},{4,6},{5,7},{6,4},{7,5},{8,10},{9,11},{10,... | collective-permute-start | bytes 571400 | tf_op jit(solution)/shard_map/ppermute | solution.py:34
  175.2 2.9 %collective-permute-start.20 = (f32[192,1536]{1,0:T(8,128)S(1)}, f32[192,1536]{1,0:T(8,128)S(1)}, u32[]{:S(2)}, u32[]{:S(2)}) collective-permute-start(f32[192,1536]{1,0:T(8,128)S(1)} %maximum_select_fusion.1), channel_id=1, source_target_pairs={{0,4},{4,0},{8,12},{12,8},{16,20},{20,16},{24,28},{28,24},{1,5},{5... | collective-permute-start | bytes 3538952 | tf_op jit(solution)/shard_map/ppermute | solution.py:71
  (68 other events, 1189.9 us)
Sparse Core Ops, SparseCore 0:
  9.6 40.3 all-gather.3
  87.9 50.2 all-gather.5
where the time goes:
time: 187 us
  waiting for transfers between devices  64.7 us (35%)
  starting transfers between devices  39.4 us (21%)
  other arithmetic  22.9 us (12%)
  blocking collectives  22.6 us (12%)
  between operations  15.7 us (8%)
  local copies, waits for them, and re-layouts  15.2 us (8%)
  matrix products  6.16 us (3%)
    all_to_all x1, blocking collectives, on_device(): lax.all_to_all(own_columns, 'tensor', split_axis=0, concat_axis=1, tiled=...  22.6 us
    ppermute x10, waiting for transfers between devices, all_sum(): x = x + lax.ppermute(x, axis, [(i, i ^ step) for i in range(peers)])  21.2 us
    all_gather x1, waiting for transfers between devices, gather_weight(): held = lax.all_gather(mine, 'tensor', axis=0, tiled=False)  14.4 us
    ppermute x5, waiting for transfers between devices, all_moments(): lax.ppermute(jnp.stack([mean, spread]), axis, [(i, i ^ step) for i in ran...  10.9 us
    ppermute x10, starting transfers between devices, all_sum(): x = x + lax.ppermute(x, axis, [(i, i ^ step) for i in range(peers)])  10.4 us
    ppermute x2, starting transfers between devices, extended(): before = lax.ppermute(last, axis, up)  9.48 us
    another operation x32, local copies, waits for them, and re-layouts, on_device(): jnp.stack([jnp.sum(padded[:, offset:offset + frames, :].astype(jnp.float3...  7.97 us
    ppermute x5, starting transfers between devices, all_moments(): lax.ppermute(jnp.stack([mean, spread]), axis, [(i, i ^ step) for i in ran...  7.35 us
  transfers between devices with their start and end apart: 29, of which 19 were waited for; matrix products, arithmetic and copies ran while one was open for 18% of the time, Pallas kernels for 0%

commit v1 on v0

--- a/solution.py
+++ b/solution.py
@@ -4,6 +4,28 @@
 from jax.sharding import PartitionSpec as P
 
 epsilon = 1e-05
+
+
+def laid_out(tiles, dim):
+    shape = list(tiles.shape[1:])
+    shape[dim] *= tiles.shape[0]
+    return jnp.moveaxis(tiles, 0, dim).reshape(shape)
+
+
+def ring_gather(x, axis, dim):
+    size = lax.axis_size(axis)
+    pairs = [(i, (i + 1) % size) for i in range(size)]
+    back = [(b, a) for a, b in pairs]
+    lower, upper = ([], [])
+    for step in range(size - 1):
+        if step % 2 == 0:
+            lower.append(lax.ppermute(lower[-1] if lower else x, axis, pairs))
+        else:
+            upper.append(lax.ppermute(upper[-1] if upper else x, axis, back))
+    tiles = jnp.stack([*lower[::-1], x, *upper])
+    shift = lax.axis_index(axis) - len(lower)
+    tiles = tiles[(jnp.arange(size) - shift) % size]
+    return laid_out(tiles, dim)
 
 
 def extended(array, sides, width):
@@ -98,7 +120,7 @@
     local = glu_input.shape[0] * frames
     everyone = local * lax.axis_size("dp") * peers
     flat_grad = out_grad.reshape(-1, width)
-    group_grad = lax.all_gather(flat_grad, "tensor", axis=0, tiled=True)
+    group_grad = ring_gather(flat_grad, "tensor", 0)
     values = glu_input[..., :width].astype(jnp.float32)
     gates = jax.nn.sigmoid(glu_input[..., width:].astype(jnp.float32))
     gated = (values * gates).astype(jnp.bfloat16)

time: 187 us -> 209 us (1.12)
  waiting for transfers between devices: 64.7 us -> 82.6 us
  other arithmetic: 22.9 us -> 29.9 us
  local copies, waits for them, and re-layouts: 15.2 us -> 12.2 us
    ppermute x0 -> x3, waiting for transfers between devices: none -> 9.31 us  [the longest x2 9.31 us: ring_gather(): lower.append(lax.ppermute(lower[-1] if lower else x, axis, pairs))]
    ppermute x3, waiting for transfers between devices: 1.12 us -> 10.2 us  [rows_sum(): x = keep + lax.ppermute(give, axis, [(i, i ^ step) for i in range(peers)])]
    another operation x32, local copies, waits for them, and re-layouts: 7.97 us -> 0.52 us  [on_device(): jnp.stack([jnp.sum(padded[:, offset:offset + frames, :].astype(jnp.float3...]
    ppermute x5, waiting for transfers between devices: 10.9 us -> 17.5 us  [all_moments(): lax.ppermute(jnp.stack([mean, spread]), axis, [(i, i ^ step) for i in ran...]
    all_gather x1 -> x0, waiting for transfers between devices: 5.77 us -> none  [on_device(): group_grad = lax.all_gather(flat_grad, 'tensor', axis=0, tiled=True)]
    another operation x2 -> x3, other arithmetic: 4.36 us -> 10 us
    ppermute x3, waiting for transfers between devices: 6.13 us -> 1.06 us  [rows_sum(): other = lax.ppermute(x, axis, [(i, i ^ step) for i in range(peers)])]
    ppermute x10, starting transfers between devices: 10.4 us -> 6.5 us  [all_sum(): x = x + lax.ppermute(x, axis, [(i, i ^ step) for i in range(peers)])]
  transfers between devices with their start and end apart: 29 -> 31, of which waited for: 19 -> 18; matrix products, arithmetic and copies ran while one was open for 18% -> 12% of each run, Pallas kernels for 0% -> 0%
where the time goes in v1:
time: 209 us; the launch traced here: 208 us
  waiting for transfers between devices  82.6 us (40%)
  starting transfers between devices  40.4 us (19%)
  other arithmetic  29.9 us (14%)
  blocking collectives  21.5 us (10%)
  between operations  15.4 us (7%)
  local copies, waits for them, and re-layouts  12.2 us (6%)
  matrix products  6.15 us (3%)
    ppermute x10, waiting for transfers between devices, all_sum(): x = x + lax.ppermute(x, axis, [(i, i ^ step) for i in range(peers)])  24.2 us
    all_to_all x1, blocking collectives, on_device(): lax.all_to_all(own_columns, 'tensor', split_axis=0, concat_axis=1, tiled=...  21.5 us
    ppermute x5, waiting for transfers between devices, all_moments(): lax.ppermute(jnp.stack([mean, spread]), axis, [(i, i ^ step) for i in ran...  17.5 us
    all_gather x1, waiting for transfers between devices, gather_weight(): held = lax.all_gather(mine, 'tensor', axis=0, tiled=False)  15.7 us
    ppermute x3, waiting for transfers between devices, rows_sum(): x = keep + lax.ppermute(give, axis, [(i, i ^ step) for i in range(peers)])  10.2 us
    ppermute x2, starting transfers between devices, extended(): before = lax.ppermute(last, axis, up)  10.1 us
    ppermute x2, waiting for transfers between devices, ring_gather(): lower.append(lax.ppermute(lower[-1] if lower else x, axis, pairs))  9.31 us
    ppermute x5, starting transfers between devices, all_moments(): lax.ppermute(jnp.stack([mean, spread]), axis, [(i, i ^ step) for i in ran...  8.3 us
  transfers between devices with their start and end apart: 31, of which 18 were waited for; matrix products, arithmetic and copies ran while one was open for 12% of the time, Pallas kernels for 0%

profile of v1, /device:TPU:0, one launch (start us, length us, event | category | flops | bytes accessed | tf_op | source)
XLA Modules:
  0.0 208.1 jit_solution(18041520989941999849)
XLA Ops:
  8.7 4.9 %collective-permute-start = (bf16[2,15,1536]{2,1,0:T(8,128)(2,1)S(1)}, bf16[2,15,1536]{2,1,0:T(8,128)(2,1)S(1)}, u32[]{:S(2)}, u32[]{:S(2)}) collective-permute-start(bf16[2,15,1536]{2,1,0:T(8,128)(2,1)S(1)} %get-tuple-element.99), channel_id=1, source_target_pairs={{0,1},{1,2},{2,3},{4,5},{5,6},{6,7},{8,9},{9,10},{10,11},{12,13},{... | collective-permute-start | bytes 276488 | tf_op jit(solution)/shard_map/ppermute | solution.py:38
  15.9 4.4 %collective-permute-done.1 = bf16[2,15,1536]{2,1,0:T(8,128)(2,1)S(1)} collective-permute-done((bf16[2,15,1536]{2,1,0:T(8,128)(2,1)S(1)}, bf16[2,15,1536]{2,1,0:T(8,128)(2,1)S(1)}, u32[]{:S(2)}, u32[]{:S(2)}) %collective-permute-start.1) | collective-permute-done | bytes 92192 | tf_op jit(solution)/shard_map/ppermute | solution.py:39
  20.3 3.8 %fusion.145 = (f32[1536]{0:T(1024)S(1)}, f32[2,64,1536]{2,1,0:T(8,128)S(1)}) fusion(bf16[2,15,1536]{2,1,0:T(8,128)(2,1)S(1)} %collective-permute-done.1, bf16[2,64,1536]{2,1,0:T(8,128)(2,1)S(1)} %fusion, f32[1536]{0:T(1024)S(1)} %get-tuple-element.72, f32[1536]{0:T(1024)S(1)} %get-tuple-element.73, f32[1536]{0:T(1024)S(1)} %get-tuple-element.44, ...), kind=kLoop, calls=%fused_computation.389 | loop fusion | flops 35977728 | bytes 1560576 | tf_op jit(solution)/shard_map/reduce_sum | solution.py:131
  25.6 1.6 collective-permute-start.6
  27.2 2.2 %collective-permute-done.6 = f32[2,1536]{1,0:T(2,128)S(1)} collective-permute-done((f32[2,1536]{1,0:T(2,128)S(1)}, f32[2,1536]{1,0:T(2,128)S(1)}, u32[]{:S(2)}, u32[]{:S(2)}) %collective-permute-start.6) | collective-permute-done | bytes 12320 | tf_op jit(solution)/shard_map/ppermute | solution.py:66
  29.4 1.6 collective-permute-start.7
  31.3 1.7 collective-permute-start.4
  33.5 1.6 collective-permute-start.8
  35.1 13.9 %collective-permute-done.8 = f32[2,1536]{1,0:T(2,128)S(1)} collective-permute-done((f32[2,1536]{1,0:T(2,128)S(1)}, f32[2,1536]{1,0:T(2,128)S(1)}, u32[]{:S(2)}, u32[]{:S(2)}) %collective-permute-start.8) | collective-permute-done | bytes 12320 | tf_op jit(solution)/shard_map/ppermute | solution.py:66
  49.1 3.4 %collective-permute-start.9 = (f32[2,1536]{1,0:T(2,128)S(1)}, f32[2,1536]{1,0:T(2,128)S(1)}, u32[]{:S(2)}, u32[]{:S(2)}) collective-permute-start(f32[2,1536]{1,0:T(2,128)S(1)} %pad_maximum_fusion.11), channel_id=1, source_target_pairs={{0,2},{1,3},{2,0},{3,1},{4,6},{5,7},{6,4},{7,5},{8,10},{9,11},{10,... | collective-permute-start | bytes 36872 | tf_op jit(solution)/shard_map/ppermute | solution.py:66
  54.9 9.3 %collective-permute-done.3 = bf16[128,1536]{1,0:T(8,128)(2,1)S(1)} collective-permute-done((bf16[128,1536]{1,0:T(8,128)(2,1)}, bf16[128,1536]{1,0:T(8,128)(2,1)S(1)}, u32[]{:S(2)}, u32[]{:S(2)}) %collective-permute-start.3) | collective-permute-done | bytes 393248 | tf_op jit(solution)/shard_map/ppermute | solution.py:22
  64.2 2.3 %pad_maximum_fusion.1 = bf16[4,128,1536]{2,1,0:T(8,128)(2,1)} fusion(bf16[1,128,1536]{2,1,0:T(8,128)(2,1)S(1)} %bitcast.34, bf16[1,128,1536]{2,1,0:T(8,128)(2,1)S(1)} %bitcast.33, bf16[1,128,1536]{2,1,0:T(8,128)(2,1)} %bitcast.2, bf16[1,128,1536]{2,1,0:T(8,128)(2,1)S(1)} %bitcast.35), kind=kLoop, calls=%fused_computation.94 | loop fusion | flops 2359296 | bytes 3145728 | tf_op jit(solution)/shard_map/stack | solution.py:25
  66.5 3.2 %gather_fusion = bf16[4,128,1536]{2,1,0:T(8,128)(2,1)} fusion(bf16[4,128,1536]{2,1,0:T(8,128)(2,1)} %pad_maximum_fusion.1, s32[1024]{0:T(1024)S(1)} %pad_clamp_fusion), kind=kCustom, calls=%fused_computation | custom fusion | bytes 3145744 | tf_op jit(solution)/shard_map/gather | solution.py:27
  69.8 2.4 %fusion.149 = f32[512,384]{1,0:T(8,128)S(1)} fusion(bf16[512,1536]{1,0:T(8,128)(2,1)} %bitcast.24, bf16[384,1536]{1,0:T(8,128)(2,1)S(1)} %copy-done), kind=kOutput, calls=%fused_computation.392 | convolution fusion | flops 603979776 | bytes 3538944 | tf_op jit(solution)/shard_map/fd,cd->fc/dot_general | solution.py:142
  72.2 21.5 %all_to_all.35 = f32[4,128,384]{2,1,0:T(8,128)S(1)} all-to-all(f32[4,128,384]{2,1,0:T(8,128)S(1)} %bitcast.30), channel_id=1, replica_groups=mesh['dp'=8,'tensor'=4] {'tensor'}, dimensions={0} | all-to-all | bytes 1572864 | tf_op jit(solution)/shard_map/all_to_all | solution.py:145
  95.3 2.5 %fusion.142 = (f32[1536]{0:T(1024)S(1)}, f32[1536]{0:T(1024)S(1)}, f32[2,64,1536]{2,1,0:T(8,128)}, bf16[2,64,1536]{2,1,0:T(8,128)(2,1)S(1)}) fusion(f32[1536]{0:T(1024)} %get-tuple-element.90, f32[2,64,1536]{2,1,0:T(8,128)S(1)} %get-tuple-element.93, f32[1536]{0:T(1024)} %get-tuple-element.8, f32[2,64,1536]{2,1,0:T(8,128)} %reshape.242, f32[1536]{0:T(1024)} %param.9, ...), kind=kLoop, calls=%fused_computation.387 | loop fusion | flops 3142656 | bytes 2789376 | tf_op jit(solution)/shard_map/reduce_sum | solution.py:158
  98.1 3.5 %collective-permute-done.11 = f32[2,1536]{1,0:T(2,128)S(1)} collective-permute-done((f32[2,1536]{1,0:T(2,128)S(1)}, f32[2,1536]{1,0:T(2,128)S(1)}, u32[]{:S(2)}, u32[]{:S(2)}) %collective-permute-start.11) | collective-permute-done | bytes 12320 | tf_op jit(solution)/shard_map/ppermute | solution.py:56
  102.8 4.0 %all-to-all-start.1 = ((bf16[128,4,384]{2,0,1:T(8,128)(2,1)}), bf16[128,4,384]{2,0,1:T(8,128)(2,1)S(1)}, u32[]{:S(2)}, u32[]{:S(2)}) async-start(bf16[128,4,384]{2,0,1:T(8,128)(2,1)} %copy.17), calls=%async_computation.1 | async-start | bytes 786432 | tf_op jit(solution)/shard_map/all_to_all | solution.py:154
  108.1 1.6 collective-permute-start.14
  109.6 2.2 %collective-permute-done.14 = f32[2,1536]{1,0:T(2,128)S(1)} collective-permute-done((f32[2,1536]{1,0:T(2,128)S(1)}, f32[2,1536]{1,0:T(2,128)S(1)}, u32[]{:S(2)}, u32[]{:S(2)}) %collective-permute-start.14) | collective-permute-done | bytes 12320 | tf_op jit(solution)/shard_map/ppermute | solution.py:56
  113.3 2.3 %collective-permute-done.15 = f32[2,1536]{1,0:T(2,128)S(1)} collective-permute-done((f32[2,1536]{1,0:T(2,128)S(1)}, f32[2,1536]{1,0:T(2,128)S(1)}, u32[]{:S(2)}, u32[]{:S(2)}) %collective-permute-start.15) | collective-permute-done | bytes 12320 | tf_op jit(solution)/shard_map/ppermute | solution.py:56
  115.9 2.2 %fusion.150 = f32[384,1536]{1,0:T(8,128)S(1)} fusion(bf16[512,384]{1,0:T(8,128)(2,1)S(1)} %bitcast.29, bf16[512,1536]{1,0:T(8,128)(2,1)} %bitcast.25), kind=kOutput, calls=%fused_computation.393 | convolution fusion | flops 603979776 | bytes 4325376 | tf_op jit(solution)/shard_map/fc,fd->cd/dot_general | solution.py:155
  119.2 1.6 fusion.80
  123.2 1.6 collective-permute-start.19
  129.3 10.2 %collective-permute-done.19 = f32[96,1536]{1,0:T(8,128)} collective-permute-done((f32[96,1536]{1,0:T(8,128)S(1)}, f32[96,1536]{1,0:T(8,128)}, u32[]{:S(2)}, u32[]{:S(2)}) %collective-permute-start.19) | collective-permute-done | bytes 589856 | tf_op jit(solution)/shard_map/ppermute | solution.py:89
  144.9 5.2 %collective-permute-start.17 = (bf16[2,15,1536]{2,1,0:T(8,128)(2,1)}, bf16[2,15,1536]{2,1,0:T(8,128)(2,1)}, u32[]{:S(2)}, u32[]{:S(2)}) collective-permute-start(bf16[2,15,1536]{2,1,0:T(8,128)(2,1)} %get-tuple-element.98), channel_id=1, source_target_pairs={{0,1},{1,2},{2,3},{4,5},{5,6},{6,7},{8,9},{9,10},{10,11},{12,13},{... | collective-permute-start | bytes 276488 | tf_op jit(solution)/shard_map/ppermute | solution.py:38
  150.1 1.6 collective-permute-start.26
  151.7 15.7 %all-gather.3.cloned.1.call-done = bf16[768,1536]{1,0:T(8,128)(2,1)} async-done(((bf16[192,1536]{1,0:T(8,128)(2,1)}), bf16[768,1536]{1,0:T(8,128)(2,1)}) %all-gather.3.cloned.1.call-update) | async-done | bytes 2359312 | tf_op jit(solution)/shard_map/all_gather | solution.py:105
  170.0 7.4 %multiply_convert_fusion = (bf16[2,64,1536]{2,1,0:T(8,128)(2,1)S(1)}, f32[2,64,1536]{2,1,0:T(8,128)S(1)}) fusion(bf16[2,64,3072]{2,1,0:T(8,128)(2,1)S(1)} %copy-done.1, bf16[2,64,1536]{2,1,0:T(8,128)(2,1)S(1)} %get-tuple-element.86, bf16[2,15,1536]{2,1,0:T(8,128)(2,1)} %collective-permute-done.17, f32[1536]{0:T(1024)} %copy-done.41, f32[1536]{0:T(1024)} %copy-done.42, ...), kind=kLoop, calls=%fused_computation.212 | loop fusion | flops 36962304 | bytes 2340864 | tf_op jit(solution)/shard_map/convert
  179.8 4.7 %collective-permute-done.27 = f32[31,1536]{1,0:T(8,128)S(1)} collective-permute-done((f32[31,1536]{1,0:T(8,128)S(1)}, f32[31,1536]{1,0:T(8,128)S(1)}, u32[]{:S(2)}, u32[]{:S(2)}) %collective-permute-start.27) | collective-permute-done | bytes 190496 | tf_op jit(solution)/shard_map/ppermute | solution.py:56
  186.9 9.0 %collective-permute-done.28 = f32[31,1536]{1,0:T(8,128)S(1)} collective-permute-done((f32[31,1536]{1,0:T(8,128)S(1)}, f32[31,1536]{1,0:T(8,128)S(1)}, u32[]{:S(2)}, u32[]{:S(2)}) %collective-permute-start.28) | collective-permute-done | bytes 190496 | tf_op jit(solution)/shard_map/ppermute | solution.py:56
  199.7 1.6 maximum_select_fusion
  (225 shorter events, 38.2 us)
Async XLA Ops:
  7.2 62.6 %copy-start = (bf16[384,1536]{1,0:T(8,128)(2,1)S(1)}, bf16[384,1536]{1,0:T(8,128)(2,1)}, u32[]{:S(2)}) copy-start(bf16[384,1536]{1,0:T(8,128)(2,1)} %param.10) | copy-start | bytes 3538948
  8.7 7.2 %collective-permute-start = (bf16[2,15,1536]{2,1,0:T(8,128)(2,1)S(1)}, bf16[2,15,1536]{2,1,0:T(8,128)(2,1)S(1)}, u32[]{:S(2)}, u32[]{:S(2)}) collective-permute-start(bf16[2,15,1536]{2,1,0:T(8,128)(2,1)S(1)} %get-tuple-element.99), channel_id=1, source_target_pairs={{0,1},{1,2},{2,3},{4,5},{5,6},{6,7},{8,9},{9,10},{10,11},{12,13},{... | collective-permute-start | bytes 276488 | tf_op jit(solution)/shard_map/ppermute | solution.py:38
  13.6 6.6 %collective-permute-start.1 = (bf16[2,15,1536]{2,1,0:T(8,128)(2,1)S(1)}, bf16[2,15,1536]{2,1,0:T(8,128)(2,1)S(1)}, u32[]{:S(2)}, u32[]{:S(2)}) collective-permute-start(bf16[2,15,1536]{2,1,0:T(8,128)(2,1)S(1)} %get-tuple-element.100), channel_id=1, source_target_pairs={{1,0},{2,1},{3,2},{5,4},{6,5},{7,6},{9,8},{10,9},{11,10},{13,12},{... | collective-permute-start | bytes 276488 | tf_op jit(solution)/shard_map/ppermute | solution.py:39
  24.3 1.2 collective-permute-start.5
  25.6 3.8 %collective-permute-start.6 = (f32[2,1536]{1,0:T(2,128)S(1)}, f32[2,1536]{1,0:T(2,128)S(1)}, u32[]{:S(2)}, u32[]{:S(2)}) collective-permute-start(f32[2,1536]{1,0:T(2,128)S(1)} %pad_maximum_fusion.8), channel_id=1, source_target_pairs={{0,8},{4,12},{8,0},{12,4},{16,24},{20,28},{24,16},{28,20},{1,9},{5... | collective-permute-start | bytes 36872 | tf_op jit(solution)/shard_map/ppermute | solution.py:66
  29.4 3.9 %collective-permute-start.7 = (f32[2,1536]{1,0:T(2,128)S(1)}, f32[2,1536]{1,0:T(2,128)S(1)}, u32[]{:S(2)}, u32[]{:S(2)}) collective-permute-start(f32[2,1536]{1,0:T(2,128)S(1)} %pad_maximum_fusion.9), channel_id=1, source_target_pairs={{0,16},{4,20},{8,24},{12,28},{16,0},{20,4},{24,8},{28,12},{1,17},{... | collective-permute-start | bytes 36872 | tf_op jit(solution)/shard_map/ppermute | solution.py:66
  31.3 23.6 %collective-permute-start.4 = (bf16[128,1536]{1,0:T(8,128)(2,1)S(1)}, bf16[128,1536]{1,0:T(8,128)(2,1)S(1)}, u32[]{:S(2)}, u32[]{:S(2)}) collective-permute-start(bf16[128,1536]{1,0:T(8,128)(2,1)S(1)} %bitcast.31), channel_id=1, source_target_pairs={{1,0},{2,1},{3,2},{0,3},{5,4},{6,5},{7,6},{4,7},{9,8},{10,9},{11,1... | collective-permute-start | bytes 1179656 | tf_op jit(solution)/shard_map/ppermute | solution.py:24
  33.0 19.5 %collective-permute-start.2 = (bf16[128,1536]{1,0:T(8,128)(2,1)S(1)}, bf16[128,1536]{1,0:T(8,128)(2,1)}, u32[]{:S(2)}, u32[]{:S(2)}) collective-permute-start(bf16[128,1536]{1,0:T(8,128)(2,1)S(1)} %bitcast.32), channel_id=1, source_target_pairs={{0,1},{1,2},{2,3},{3,0},{4,5},{5,6},{6,7},{7,4},{8,9},{9,10},{10,1... | collective-permute-start | bytes 1179656 | tf_op jit(solution)/shard_map/ppermute | solution.py:22
  33.5 15.6 %collective-permute-start.8 = (f32[2,1536]{1,0:T(2,128)S(1)}, f32[2,1536]{1,0:T(2,128)S(1)}, u32[]{:S(2)}, u32[]{:S(2)}) collective-permute-start(f32[2,1536]{1,0:T(2,128)S(1)} %pad_maximum_fusion.10), channel_id=1, source_target_pairs={{0,1},{1,0},{2,3},{3,2},{4,5},{5,4},{6,7},{7,6},{8,9},{9,8},{10,11... | collective-permute-start | bytes 36872 | tf_op jit(solution)/shard_map/ppermute | solution.py:66
  49.1 5.1 %collective-permute-start.9 = (f32[2,1536]{1,0:T(2,128)S(1)}, f32[2,1536]{1,0:T(2,128)S(1)}, u32[]{:S(2)}, u32[]{:S(2)}) collective-permute-start(f32[2,1536]{1,0:T(2,128)S(1)} %pad_maximum_fusion.11), channel_id=1, source_target_pairs={{0,2},{1,3},{2,0},{3,1},{4,6},{5,7},{6,4},{7,5},{8,10},{9,11},{10,... | collective-permute-start | bytes 36872 | tf_op jit(solution)/shard_map/ppermute | solution.py:66
  52.5 11.7 %collective-permute-start.3 = (bf16[128,1536]{1,0:T(8,128)(2,1)}, bf16[128,1536]{1,0:T(8,128)(2,1)S(1)}, u32[]{:S(2)}, u32[]{:S(2)}) collective-permute-start(bf16[128,1536]{1,0:T(8,128)(2,1)} %collective-permute-done.2), channel_id=1, source_target_pairs={{0,1},{1,2},{2,3},{3,0},{4,5},{5,6},{6,7},{7,4},{8,9},{9,10},{10,1... | collective-permute-start | bytes 1179656 | tf_op jit(solution)/shard_map/ppermute | solution.py:22
  97.9 3.8 %collective-permute-start.11 = (f32[2,1536]{1,0:T(2,128)S(1)}, f32[2,1536]{1,0:T(2,128)S(1)}, u32[]{:S(2)}, u32[]{:S(2)}) collective-permute-start(f32[2,1536]{1,0:T(2,128)S(1)} %pad_maximum_fusion.12), channel_id=1, source_target_pairs={{0,1},{1,0},{2,3},{3,2},{4,5},{5,4},{6,7},{7,6},{8,9},{9,8},{10,11... | collective-permute-start | bytes 36872 | tf_op jit(solution)/shard_map/ppermute | solution.py:56
  101.6 5.2 %collective-permute-start.12 = (f32[2,1536]{1,0:T(2,128)S(1)}, f32[2,1536]{1,0:T(2,128)S(1)}, u32[]{:S(2)}, u32[]{:S(2)}) collective-permute-start(f32[2,1536]{1,0:T(2,128)S(1)} %fusion.141), channel_id=1, source_target_pairs={{0,2},{1,3},{2,0},{3,1},{4,6},{5,7},{6,4},{7,5},{8,10},{9,11},{10,... | collective-permute-start | bytes 36872 | tf_op jit(solution)/shard_map/ppermute | solution.py:56
  102.8 13.0 %all-to-all-start.1 = ((bf16[128,4,384]{2,0,1:T(8,128)(2,1)}), bf16[128,4,384]{2,0,1:T(8,128)(2,1)S(1)}, u32[]{:S(2)}, u32[]{:S(2)}) async-start(bf16[128,4,384]{2,0,1:T(8,128)(2,1)} %copy.17), calls=%async_computation.1 | async-start | bytes 786432 | tf_op jit(solution)/shard_map/all_to_all | solution.py:154
  106.8 60.6 %all-gather.3.cloned.1.call-start = ((), (), s32[]{:S(2)}) async-start(), calls=%async_computation.2 | async-start | bytes 2949120 | tf_op jit(solution)/shard_map/all_gather | solution.py:105
  106.8 1.2 collective-permute-start.13
  108.1 3.8 %collective-permute-start.14 = (f32[2,1536]{1,0:T(2,128)S(1)}, f32[2,1536]{1,0:T(2,128)S(1)}, u32[]{:S(2)}, u32[]{:S(2)}) collective-permute-start(f32[2,1536]{1,0:T(2,128)S(1)} %add.522), channel_id=1, source_target_pairs={{0,8},{4,12},{8,0},{12,4},{16,24},{20,28},{24,16},{28,20},{1,9},{5... | collective-permute-start | bytes 36872 | tf_op jit(solution)/shard_map/ppermute | solution.py:56
  111.9 3.8 %collective-permute-start.15 = (f32[2,1536]{1,0:T(2,128)S(1)}, f32[2,1536]{1,0:T(2,128)S(1)}, u32[]{:S(2)}, u32[]{:S(2)}) collective-permute-start(f32[2,1536]{1,0:T(2,128)S(1)} %add.523), channel_id=1, source_target_pairs={{0,16},{4,20},{8,24},{12,28},{16,0},{20,4},{24,8},{28,12},{1,17},{... | collective-permute-start | bytes 36872 | tf_op jit(solution)/shard_map/ppermute | solution.py:56
  118.2 3.8 %collective-permute-start.18 = (f32[192,1536]{1,0:T(8,128)S(1)}, f32[192,1536]{1,0:T(8,128)S(1)}, u32[]{:S(2)}, u32[]{:S(2)}) collective-permute-start(f32[192,1536]{1,0:T(8,128)S(1)} %constant_dynamic-slice_fusion.2), channel_id=1, source_target_pairs={{0,4},{4,0},{8,12},{12,8},{16,20},{20,16},{24,28},{28,24},{1,5},{5... | collective-permute-start | bytes 3538952 | tf_op jit(solution)/shard_map/ppermute | solution.py:89
  123.2 16.3 %collective-permute-start.19 = (f32[96,1536]{1,0:T(8,128)S(1)}, f32[96,1536]{1,0:T(8,128)}, u32[]{:S(2)}, u32[]{:S(2)}) collective-permute-start(f32[96,1536]{1,0:T(8,128)S(1)} %constant_dynamic-slice_fusion.1), channel_id=1, source_target_pairs={{0,8},{4,12},{8,0},{12,4},{16,24},{20,28},{24,16},{28,20},{1,9},{5... | collective-permute-start | bytes 1769480 | tf_op jit(solution)/shard_map/ppermute | solution.py:89
  127.2 1.5 collective-permute-start.24
  128.7 21.4 %collective-permute-start.25 = (f32[31,1536]{1,0:T(8,128)S(1)}, f32[31,1536]{1,0:T(8,128)S(1)}, u32[]{:S(2)}, u32[]{:S(2)}) collective-permute-start(f32[31,1536]{1,0:T(8,128)S(1)} %add.563), channel_id=1, source_target_pairs={{0,8},{4,12},{8,0},{12,4},{16,24},{20,28},{24,16},{28,20},{1,9},{5... | collective-permute-start | bytes 571400 | tf_op jit(solution)/shard_map/ppermute | solution.py:56
  142.4 25.0 %collective-permute-start.20 = (f32[48,1536]{1,0:T(8,128)}, f32[48,1536]{1,0:T(8,128)}, u32[]{:S(2)}, u32[]{:S(2)}) collective-permute-start(f32[48,1536]{1,0:T(8,128)} %constant_dynamic-slice_fusion), channel_id=1, source_target_pairs={{0,16},{4,20},{8,24},{12,28},{16,0},{20,4},{24,8},{28,12},{1,17},{... | collective-permute-start | bytes 884744 | tf_op jit(solution)/shard_map/ppermute | solution.py:89
  143.6 26.4 %collective-permute-start.16 = (bf16[2,15,1536]{2,1,0:T(8,128)(2,1)}, bf16[2,15,1536]{2,1,0:T(8,128)(2,1)}, u32[]{:S(2)}, u32[]{:S(2)}) collective-permute-start(bf16[2,15,1536]{2,1,0:T(8,128)(2,1)} %get-tuple-element.97), channel_id=1, source_target_pairs={{1,0},{2,1},{3,2},{5,4},{6,5},{7,6},{9,8},{10,9},{11,10},{13,12},{... | collective-permute-start | bytes 276488 | tf_op jit(solution)/shard_map/ppermute | solution.py:39
  144.9 25.1 %collective-permute-start.17 = (bf16[2,15,1536]{2,1,0:T(8,128)(2,1)}, bf16[2,15,1536]{2,1,0:T(8,128)(2,1)}, u32[]{:S(2)}, u32[]{:S(2)}) collective-permute-start(bf16[2,15,1536]{2,1,0:T(8,128)(2,1)} %get-tuple-element.98), channel_id=1, source_target_pairs={{0,1},{1,2},{2,3},{4,5},{5,6},{6,7},{8,9},{9,10},{10,11},{12,13},{... | collective-permute-start | bytes 276488 | tf_op jit(solution)/shard_map/ppermute | solution.py:38
  150.1 27.3 %collective-permute-start.26 = (f32[31,1536]{1,0:T(8,128)S(1)}, f32[31,1536]{1,0:T(8,128)S(1)}, u32[]{:S(2)}, u32[]{:S(2)}) collective-permute-start(f32[31,1536]{1,0:T(8,128)S(1)} %add.564), channel_id=1, source_target_pairs={{0,16},{4,20},{8,24},{12,28},{16,0},{20,4},{24,8},{28,12},{1,17},{... | collective-permute-start | bytes 571400 | tf_op jit(solution)/shard_map/ppermute | solution.py:56
  167.4 29.5 %collective-permute-start.10 = (bf16[4,192,1536]{2,1,0:T(8,128)(2,1)}, bf16[4,192,1536]{2,1,0:T(8,128)(2,1)S(1)}, u32[]{:S(2)}, u32[]{:S(2)}) collective-permute-start(bf16[4,192,1536]{2,1,0:T(8,128)(2,1)} %bitcast.27), channel_id=1, source_target_pairs={{0,4},{4,0},{8,12},{12,8},{16,20},{20,16},{24,28},{28,24},{1,5},{5... | collective-permute-start | bytes 7077896 | tf_op jit(solution)/shard_map/ppermute | solution.py:106
  168.5 9.5 %collective-permute-start.21 = (f32[48,1536]{1,0:T(8,128)S(1)}, f32[48,1536]{1,0:T(8,128)S(1)}, u32[]{:S(2)}, u32[]{:S(2)}) collective-permute-start(f32[48,1536]{1,0:T(8,128)S(1)} %dynamic-slice_add_fusion.2), channel_id=1, source_target_pairs={{0,16},{4,20},{8,24},{12,28},{16,0},{20,4},{24,8},{28,12},{1,17},{... | collective-permute-start | bytes 884744 | tf_op jit(solution)/shard_map/ppermute | solution.py:93
  177.4 7.1 %collective-permute-start.27 = (f32[31,1536]{1,0:T(8,128)S(1)}, f32[31,1536]{1,0:T(8,128)S(1)}, u32[]{:S(2)}, u32[]{:S(2)}) collective-permute-start(f32[31,1536]{1,0:T(8,128)S(1)} %add.565), channel_id=1, source_target_pairs={{0,1},{1,0},{2,3},{3,2},{4,5},{5,4},{6,7},{7,6},{8,9},{9,8},{10,11... | collective-permute-start | bytes 571400 | tf_op jit(solution)/shard_map/ppermute | solution.py:56
  178.0 18.7 %collective-permute-start.22 = (f32[96,1536]{1,0:T(8,128)S(1)}, f32[96,1536]{1,0:T(8,128)S(1)}, u32[]{:S(2)}, u32[]{:S(2)}) collective-permute-start(f32[96,1536]{1,0:T(8,128)S(1)} %maximum_select_fusion.2), channel_id=1, source_target_pairs={{0,8},{4,12},{8,0},{12,4},{16,24},{20,28},{24,16},{28,20},{1,9},{5... | collective-permute-start | bytes 1769480 | tf_op jit(solution)/shard_map/ppermute | solution.py:93
  184.6 11.4 %collective-permute-start.28 = (f32[31,1536]{1,0:T(8,128)S(1)}, f32[31,1536]{1,0:T(8,128)S(1)}, u32[]{:S(2)}, u32[]{:S(2)}) collective-permute-start(f32[31,1536]{1,0:T(8,128)S(1)} %add.566), channel_id=1, source_target_pairs={{0,2},{1,3},{2,0},{3,1},{4,6},{5,7},{6,4},{7,5},{8,10},{9,11},{10,... | collective-permute-start | bytes 571400 | tf_op jit(solution)/shard_map/ppermute | solution.py:56
  196.7 2.9 %collective-permute-start.23 = (f32[192,1536]{1,0:T(8,128)S(1)}, f32[192,1536]{1,0:T(8,128)S(1)}, u32[]{:S(2)}, u32[]{:S(2)}) collective-permute-start(f32[192,1536]{1,0:T(8,128)S(1)} %maximum_select_fusion.1), channel_id=1, source_target_pairs={{0,4},{4,0},{8,12},{12,8},{16,20},{20,16},{24,28},{28,24},{1,5},{5... | collective-permute-start | bytes 3538952 | tf_op jit(solution)/shard_map/ppermute | solution.py:93
  (46 other events, 663.5 us)
Sparse Core Ops, SparseCore 0:
  113.4 53.8 all-gather.2
